TPU v7x, 256 devices: a whole 4x4x8 slice. The times are simulated.
256 devices in a mesh: ctx: 64 (over z, y_hi, x), head: 4 (over y_lo, core).
Axes of the slice: x: 4, y: 4 (y_hi: 2, y_lo: 2; y = y_hi * 2 + y_lo), z: 8, core: 2. Of those that a mesh axis runs over, the one named last changes fastest.
Arguments:
- query_rows: bfloat16 [32768, 5120], P(('ctx', 'head')), may hold values from -6 to 6
- key_rows: bfloat16 [32768, 1024], P(('ctx', 'head')), may hold values from -6 to 6
- value_rows: bfloat16 [32768, 1024], P(('ctx', 'head')), may hold values from -6 to 6
- attn_output: bfloat16 [32768, 5120], P(('ctx', 'head')), may hold values from -3 to 3
- out_grad: bfloat16 [32768, 5120], P(('ctx', 'head')), may hold values from -24 to 24
- log_norm: float32 [40, 32768], P('head', 'ctx'), may hold values from 5 to 7
- prefix_keys: bfloat16 [1024, 1024], P('ctx', 'head'), may hold values from -6 to 6
- prefix_values: bfloat16 [1024, 1024], P('ctx', 'head'), may hold values from -6 to 6
- response_blocks: int32 [128], replicated, may hold values from 1 to 16, as said below
- prompt_members: int32 [8, 16], replicated, may hold values from 0 to 127, as said below
Outputs:
- query_grad: bfloat16 [32768, 5120], P('ctx', 'head')
- key_grad: bfloat16 [32768, 1024], P('ctx', 'head')
- value_grad: bfloat16 [32768, 1024], P('ctx', 'head')
- prefix_keygrads: bfloat16 [1024, 1024], P('ctx', 'head')
- prefix_valuegrads: bfloat16 [1024, 1024], P('ctx', 'head')
Inputs may be any that keep to these rules, and one draw needn't show every extreme that they name: `response_blocks`: the lengths fill all 1024 blocks of the row. Every index of ctx from 1 on begins inside a response that started on the index before it. `prompt_members`: every response, numbered 0 to 127 in order along the row, is listed exactly once.
All inputs are finite; a program needn't handle non-finite values.
Results may differ from a plain program's by a relative error of at most 0.008.
Values may be sent and summed in bfloat16 or wider, within the bound.
No kernel may reach another device: no remote copies, remote signals or barrier semaphores. Data moves between devices by JAX's collectives and lax.ppermute only.
A program may use at most 64 MiB of HBM per device.

v0:
```python
import math
import jax
import jax.numpy as jnp
from jax import lax
from jax.sharding import PartitionSpec as P

HD = 128
BLK = 32
PL = 128


def shifted(array, axis, by):
    devices = lax.axis_size(axis)
    pairs = [(i, i + by) for i in range(devices) if 0 <= i + by < devices]
    return lax.ppermute(array, axis, pairs)


def token_tables(response_blocks, prompt_members, first_block, count):
    starts = jnp.cumsum(response_blocks) - response_blocks
    responses = response_blocks.shape[0]
    group = prompt_members.shape[1]
    listed = prompt_members.reshape(-1)
    owner = jnp.arange(listed.shape[0], dtype=jnp.int32) // group
    numbers = jnp.arange(responses, dtype=jnp.int32)
    hits = listed[:, None] == numbers[None, :]
    prompt_of = jnp.sum(jnp.where(hits, owner[:, None], 0), axis=0)
    blocks = first_block + jnp.arange(count, dtype=jnp.int32)
    before = starts[None, :] <= blocks[:, None]
    first = jnp.max(jnp.where(before, starts[None, :], 0), axis=1)
    current = jnp.sum(before.astype(jnp.int32), axis=1) - 1
    chosen = numbers[None, :] == current[:, None]
    prompt_block = jnp.sum(jnp.where(chosen, prompt_of[None, :], 0), axis=1)
    return (jnp.repeat(first * BLK, BLK), jnp.repeat(prompt_block, BLK))


def tile_terms(queries, grads, norms, deltas, keys, values, allowed):
    rows = queries.shape[0]
    cols = keys.shape[0]
    heads = norms.shape[1]
    group = heads // (keys.shape[1] // HD)
    scale = 1.0 / math.sqrt(HD)

    def one_head(head, carry):
        query_acc, key_acc, value_acc = carry
        kv_head = head // group
        query_h = lax.dynamic_slice_in_dim(queries, head * HD, HD, 1)
        grad_h = lax.dynamic_slice_in_dim(grads, head * HD, HD, 1)
        key_h = lax.dynamic_slice_in_dim(keys, kv_head * HD, HD, 1)
        value_h = lax.dynamic_slice_in_dim(values, kv_head * HD, HD, 1)
        norm_h = lax.dynamic_slice_in_dim(norms, head, 1, 1)
        delta_h = lax.dynamic_slice_in_dim(deltas, head, 1, 1)
        logits = jnp.dot(query_h, key_h.T, preferred_element_type=jnp.float32)
        weights = jnp.where(allowed, jnp.exp(logits * scale - norm_h), 0.0)
        weights_b = weights.astype(jnp.bfloat16)
        value_term = jnp.dot(weights_b.T, grad_h, preferred_element_type=jnp.float32)
        dweights = jnp.dot(grad_h, value_h.T, preferred_element_type=jnp.float32)
        dlogits = (weights * (dweights - delta_h)).astype(jnp.bfloat16)
        query_term = jnp.dot(dlogits, key_h, preferred_element_type=jnp.float32)
        key_term = jnp.dot(dlogits.T, query_h, preferred_element_type=jnp.float32)
        query_acc = lax.dynamic_update_slice_in_dim(query_acc, query_term, head * HD, 1)
        old_key = lax.dynamic_slice_in_dim(key_acc, kv_head * HD, HD, 1)
        key_acc = lax.dynamic_update_slice_in_dim(key_acc, old_key + key_term, kv_head * HD, 1)
        old_value = lax.dynamic_slice_in_dim(value_acc, kv_head * HD, HD, 1)
        value_acc = lax.dynamic_update_slice_in_dim(
            value_acc, old_value + value_term, kv_head * HD, 1
        )
        return (query_acc, key_acc, value_acc)

    start = (
        jnp.zeros((rows, queries.shape[1]), jnp.float32),
        jnp.zeros((cols, keys.shape[1]), jnp.float32),
        jnp.zeros((cols, keys.shape[1]), jnp.float32),
    )
    return lax.fori_loop(0, heads, one_head, start)


def add_rows(total, term, offset):
    old = lax.dynamic_slice_in_dim(total, offset, term.shape[0], 0)
    return lax.dynamic_update_slice_in_dim(total, old + term, offset, 0)


def shards(
    query_rows,
    key_rows,
    value_rows,
    attn_output,
    out_grad,
    log_norm,
    prefix_keys,
    prefix_values,
    response_blocks,
    prompt_members,
):
    queries, keys, values, outputs, grads = (
        lax.all_to_all(query_rows, "head", split_axis=1, concat_axis=0, tiled=True),
        lax.all_to_all(key_rows, "head", split_axis=1, concat_axis=0, tiled=True),
        lax.all_to_all(value_rows, "head", split_axis=1, concat_axis=0, tiled=True),
        lax.all_to_all(attn_output, "head", split_axis=1, concat_axis=0, tiled=True),
        lax.all_to_all(out_grad, "head", split_axis=1, concat_axis=0, tiled=True),
    )
    own_heads = queries.shape[1] // HD
    deltas = jnp.einsum(
        "thd,thd->th",
        grads.reshape(-1, own_heads, HD),
        outputs.reshape(-1, own_heads, HD),
        preferred_element_type=jnp.float32,
    )
    tokens = queries.shape[0]
    scale = 1.0 / math.sqrt(HD)
    norms = log_norm.T
    position = lax.axis_index("ctx")
    base = position * tokens
    starts, prompts = token_tables(
        response_blocks, prompt_members, position * (tokens // BLK), tokens // BLK
    )
    local_start = starts - base
    positions = jnp.arange(tokens, dtype=jnp.int32)
    allowed_here = (positions[None, :] >= local_start[:, None]) & (
        positions[None, :] <= positions[:, None]
    )
    allowed_prior = positions[None, :] - tokens >= local_start[:, None]
    query_one, key_one, value_one = tile_terms(
        queries, grads, norms, deltas, keys, values, allowed_here
    )
    keys_prior, values_prior = shifted((keys, values), "ctx", 1)
    query_two, key_two, value_two = tile_terms(
        queries, grads, norms, deltas, keys_prior, values_prior, allowed_prior
    )
    back_keys, back_values = (
        shifted(key_two.astype(jnp.bfloat16), "ctx", -1).astype(key_two.dtype),
        shifted(value_two.astype(jnp.bfloat16), "ctx", -1).astype(value_two.dtype),
    )
    whole_keys, whole_values = (
        lax.all_gather(prefix_keys, "ctx", axis=0, tiled=True),
        lax.all_gather(prefix_values, "ctx", axis=0, tiled=True),
    )
    prompt_total = whole_keys.shape[0]
    prompt_count = prompt_total // PL
    width = prefix_keys.shape[1]
    init = (
        query_one + query_two,
        jnp.zeros((prompt_total, width), jnp.float32),
        jnp.zeros((prompt_total, width), jnp.float32),
    )

    def prompt_step(number, state):
        seen = prompts == number

        def compute(inner):
            total, pkeys, pvalues = inner
            keys_p = lax.dynamic_slice_in_dim(whole_keys, number * PL, PL, 0)
            values_p = lax.dynamic_slice_in_dim(whole_values, number * PL, PL, 0)
            allowed = jnp.broadcast_to(seen[:, None], (tokens, PL))
            query_p, key_p, value_p = tile_terms(
                queries, grads, norms, deltas, keys_p, values_p, allowed
            )
            return (
                total + query_p,
                add_rows(pkeys, key_p, number * PL),
                add_rows(pvalues, value_p, number * PL),
            )

        return lax.cond(jnp.any(seen), compute, lambda inner: inner, state)

    query_total, pkey_acc, pvalue_acc = lax.fori_loop(0, prompt_count, prompt_step, init)
    pkey_sum, pvalue_sum = (
        lax.psum_scatter(pkey_acc, "ctx", scatter_dimension=0, tiled=True),
        lax.psum_scatter(pvalue_acc, "ctx", scatter_dimension=0, tiled=True),
    )
    return (
        (query_total * scale).astype(jnp.bfloat16),
        ((key_one + back_keys) * scale).astype(jnp.bfloat16),
        (value_one + back_values).astype(jnp.bfloat16),
        (pkey_sum * scale).astype(jnp.bfloat16),
        pvalue_sum.astype(jnp.bfloat16),
    )


def solution(mesh):
    placed = (
        P(("ctx", "head"), None),
        P(("ctx", "head"), None),
        P(("ctx", "head"), None),
        P(("ctx", "head"), None),
        P(("ctx", "head"), None),
        P("head", "ctx"),
        P("ctx", "head"),
        P("ctx", "head"),
        P(),
        P(),
    )
    return jax.shard_map(
        shards,
        mesh=mesh,
        in_specs=placed,
        out_specs=(
            P("ctx", "head"),
            P("ctx", "head"),
            P("ctx", "head"),
            P("ctx", "head"),
            P("ctx", "head"),
        ),
        check_vma=False,
    )
```

profile of v0, /device:TPU:8, one launch (start us, length us, event | category | flops | bytes accessed | tf_op | source)
XLA Modules:
  0.0 1574.4 jit_solution(12429472949831046137)
XLA Ops:
  7.2 1.8 copy.67
  8.9 5.5 all-to-all-start.1
  14.5 1.7 copy.66
  16.2 2.7 all-to-all-done.1
  18.9 5.0 all-to-all-start.3
  23.9 1.4 copy.46
  25.3 2.9 all-to-all-done.3
  28.2 5.3 all-to-all-start.2
  33.5 1.5 copy.50
  35.0 14.1 all-to-all-done.2
  49.1 5.3 all-to-all-start.4
  54.8 2.5 copy.65
  57.7 12.3 all-to-all-done.4
  70.0 6.1 all-to-all-start
  76.3 195.1 %all_gather.6 = bf16[1024,256]{1,0:T(8,128)(2,1)} all-gather(bf16[16,256]{1,0:T(8,128)(2,1)S(1)} %copy-done.9), channel_id=1, replica_groups=mesh['ctx'=64,'head'=4] {'ctx'}, dimensions={0}, use_global_device_ids=true | all-gather | bytes 532480 | tf_op jit(solution)/shard_map/all_gather | solution.py:134
  271.4 186.6 %all_gather.7 = bf16[1024,256]{1,0:T(8,128)(2,1)} all-gather(bf16[16,256]{1,0:T(8,128)(2,1)S(1)} %copy-done.10), channel_id=1, replica_groups=mesh['ctx'=64,'head'=4] {'ctx'}, dimensions={0}, use_global_device_ids=true | all-gather | bytes 532480 | tf_op jit(solution)/shard_map/all_gather | solution.py:135
  458.1 3.9 collective-permute-start
  462.0 2.6 collective-permute-start.1
  464.7 6.9 copy.49
  471.7 3.5 reshape.101
  475.2 6.9 copy.51
  482.1 3.5 reshape.102
  485.6 1.5 copy.47
  487.0 2.3 fusion.69
  489.4 1.6 broadcast.110.clone.1
  491.1 69.6 %while.79 = (s32[]{:T(128)}, f32[512,1280]{1,0:T(8,128)}, f32[512,256]{1,0:T(8,128)S(1)}, f32[512,256]{1,0:T(8,128)S(1)}, bf16[512,1280]{1,0:T(8,128)(2,1)}, /*i...) while((s32[]{:T(128)}, f32[512,1280]{1,0:T(8,128)}, ...), condition=%wide.region_5.6_spmd.clone, body=%wide.region_4.5_spmd.clone.sunk | while | flops 337772544 | bytes 6963587 | solution.py:74
  491.9 1.3 fusion.146
  498.8 1.3 fusion.146
  505.7 1.3 fusion.146
  512.7 1.3 fusion.146
  519.7 1.3 fusion.146
  533.6 1.3 fusion.146
  540.5 1.3 fusion.146
  560.7 1.7 broadcast.110.clone
  562.5 69.3 %while.78 = (s32[]{:T(128)}, f32[512,1280]{1,0:T(8,128)}, f32[512,256]{1,0:T(8,128)S(1)}, f32[512,256]{1,0:T(8,128)S(1)}, bf16[512,1280]{1,0:T(8,128)(2,1)}, /*i...) while((s32[]{:T(128)}, f32[512,1280]{1,0:T(8,128)}, ...), condition=%wide.region_3.4_spmd.clone, body=%wide.region_2.3_spmd.clone.sunk | while | flops 338296832 | bytes 6961531 | solution.py:74
  563.2 1.3 fusion.132
  570.1 1.3 fusion.132
  577.0 1.3 fusion.132
  583.9 1.3 fusion.132
  590.9 1.3 fusion.132
  597.7 1.3 fusion.132
  604.6 1.3 fusion.132
  611.6 1.3 fusion.132
  618.5 1.3 fusion.132
  625.4 1.3 fusion.132
  631.8 4.7 add.320
  638.6 136.6 %while.80 = (s32[]{:T(128)}, f32[512,1280]{1,0:T(8,128)}, f32[1024,256]{1,0:T(8,128)}, f32[1024,256]{1,0:T(8,128)}, bf16[1024,256]{1,0:T(8,128)(2,1)}, /*index=5...) while((s32[]{:T(128)}, f32[512,1280]{1,0:T(8,128)}, ...), condition=%wide.region_15.16_spmd.clone, body=%wide.region_9.15_spmd.clone.sunk | while | flops 85099536 | bytes 14145448 | solution.py:165
  640.0 62.4 %conditional.3 = ((f32[512,1280]{1,0:T(8,128)}, f32[1024,256]{1,0:T(8,128)}, f32[1024,256]{1,0:T(8,128)})) conditional(s32[]{:T(128)} %convert_element_type.143, (f32[512,1280]{1,0:T(8,128)}, f32[1024,256]{1,0:T(8,128)}, f32[1024,256]{1,0:T(8,128)}) %tuple.159, (s32[]{:T(128)}, bf16[1024,256]{1,0:T(8,128)(2,1)}, bf16[1024,256]{1,0:T(8,128)(2,1)}, ...), branch_computations={%region_11.11_spmd, %region_12.14_spmd} | conditional | flops 85098512 | bytes 14136441 | solution.py:163
  641.9 55.2 %while.77 = (s32[]{:T(128)}, f32[512,1280]{1,0:T(8,128)S(1)}, f32[128,256]{1,0:T(8,128)S(1)}, f32[128,256]{1,0:T(8,128)S(1)}, bf16[512,1280]{1,0:T(8,128)(2,1)},...) while((s32[]{:T(128)}, f32[512,1280]{1,0:T(8,128)S(1)}, ...), condition=%wide.region_14.13_spmd.clone, body=%wide.region_13.12_spmd.clone.sunk | while | flops 84377616 | bytes 2339707 | solution.py:74
  697.2 1.7 add_dynamic-update-slice_fusion
  698.9 3.5 add.309
  711.3 62.4 %conditional.3 = ((f32[512,1280]{1,0:T(8,128)}, f32[1024,256]{1,0:T(8,128)}, f32[1024,256]{1,0:T(8,128)})) conditional(s32[]{:T(128)} %convert_element_type.143, (f32[512,1280]{1,0:T(8,128)}, f32[1024,256]{1,0:T(8,128)}, f32[1024,256]{1,0:T(8,128)}) %tuple.159, (s32[]{:T(128)}, bf16[1024,256]{1,0:T(8,128)(2,1)}, bf16[1024,256]{1,0:T(8,128)(2,1)}, ...), branch_computations={%region_11.11_spmd, %region_12.14_spmd} | conditional | flops 85098512 | bytes 14136441 | solution.py:163
  713.2 55.2 %while.77 = (s32[]{:T(128)}, f32[512,1280]{1,0:T(8,128)S(1)}, f32[128,256]{1,0:T(8,128)S(1)}, f32[128,256]{1,0:T(8,128)S(1)}, bf16[512,1280]{1,0:T(8,128)(2,1)},...) while((s32[]{:T(128)}, f32[512,1280]{1,0:T(8,128)S(1)}, ...), condition=%wide.region_14.13_spmd.clone, body=%wide.region_13.12_spmd.clone.sunk | while | flops 84377616 | bytes 2339707 | solution.py:74
  768.4 1.7 add_dynamic-update-slice_fusion
  770.1 3.5 add.309
  776.2 1.3 collective-permute-start.3
  777.6 1.3 collective-permute-start.2
  778.9 3.1 multiply_convert_fusion
  781.9 2.6 collective-permute-done.3
  785.3 2.0 collective-permute-done.2
  788.1 413.7 %reduce-scatter.5.cloned.1.call-done = f32[16,256]{1,0:T(8,128)} async-done(((f32[1024,256]{1,0:T(8,128)}), f32[16,256]{1,0:T(8,128)}) %reduce-scatter.5.cloned.1.call-update) | async-done | bytes 16400 | tf_op jit(solution)/shard_map/reduce_scatter | solution.py:168
  1201.8 1.3 convert_element_type.106
  1203.1 363.1 %reduce-scatter.3.cloned.1.call-done = f32[16,256]{1,0:T(8,128)} async-done(((f32[1024,256]{1,0:T(8,128)}), f32[16,256]{1,0:T(8,128)}) %reduce-scatter.3.cloned.1.call-update) | async-done | bytes 16400 | tf_op jit(solution)/shard_map/reduce_scatter | solution.py:167
  1566.2 1.3 multiply_convert_fusion.2
  (321 shorter events, 240.0 us)
Async XLA Ops:
  7.2 16.7 %copy-start.7 = (bf16[128,5120]{1,0:T(8,128)(2,1)S(1)}, bf16[128,5120]{1,0:T(8,128)(2,1)}, u32[]{:S(2)}) copy-start(bf16[128,5120]{1,0:T(8,128)(2,1)} %param.24) | copy-start | bytes 3932164
  8.9 9.9 all-to-all-start.1
  18.9 9.4 all-to-all-start.3
  28.2 5.3 copy-start.8
  28.2 20.9 %all-to-all-start.2 = ((bf16[128,4,1280]{0,2,1:T(8,128)(2,1)}), bf16[128,4,1280]{0,2,1:T(8,128)(2,1)S(1)}, u32[]{:S(2)}, u32[]{:S(2)}) async-start(bf16[128,4,1280]{0,2,1:T(8,128)(2,1)} %bitcast.5), calls=%async_computation.2 | async-start | bytes 2621440 | tf_op jit(solution)/shard_map/all_to_all | solution.py:99
  49.1 5.3 copy-start.12
  49.1 20.9 %all-to-all-start.4 = ((bf16[128,4,1280]{0,2,1:T(8,128)(2,1)}), bf16[128,4,1280]{0,2,1:T(8,128)(2,1)S(1)}, u32[]{:S(2)}, u32[]{:S(2)}) async-start(bf16[128,4,1280]{0,2,1:T(8,128)(2,1)} %bitcast.73), calls=%async_computation.4 | async-start | bytes 2621440 | tf_op jit(solution)/shard_map/all_to_all | solution.py:98
  54.8 2.5 copy-start.11
  70.0 6.2 copy-start.9
  70.0 201.4 %copy-start.10 = (bf16[16,256]{1,0:T(8,128)(2,1)S(1)}, bf16[16,256]{1,0:T(8,128)(2,1)}, u32[]{:S(2)}) copy-start(bf16[16,256]{1,0:T(8,128)(2,1)} %param.27) | copy-start | bytes 24580
  70.0 419.3 %all-to-all-start = ((bf16[128,4,1280]{2,0,1:T(8,128)(2,1)}), bf16[128,4,1280]{2,0,1:T(8,128)(2,1)}, u32[]{:S(2)}, u32[]{:S(2)}) async-start(bf16[128,4,1280]{2,0,1:T(8,128)(2,1)} %bitcast.72), calls=%async_computation | async-start | bytes 2621440 | tf_op jit(solution)/shard_map/all_to_all | solution.py:95
  76.1 1125.7 %reduce-scatter.5.cloned.1.call-start = ((), (), s32[]{:S(2)}) async-start(), calls=%async_computation.8 | async-start | bytes 1064960 | tf_op jit(solution)/shard_map/reduce_scatter | solution.py:168
  458.1 31.3 %collective-permute-start = (bf16[512,256]{1,0:T(8,128)(2,1)S(1)}, bf16[512,256]{1,0:T(8,128)(2,1)S(1)}, u32[]{:S(2)}, u32[]{:S(2)}) collective-permute-start(bf16[512,256]{1,0:T(8,128)(2,1)S(1)} %bitcast.75), channel_id=1, source_target_pairs={{0,4},{4,8},{8,12},{12,16},{16,20},{20,24},{24,28},{28,32},{32,36}... | collective-permute-start | bytes 786440 | tf_op jit(solution)/shard_map/ppermute | solution.py:15
  462.0 27.4 %collective-permute-start.1 = (bf16[512,256]{1,0:T(8,128)(2,1)S(1)}, bf16[512,256]{1,0:T(8,128)(2,1)}, u32[]{:S(2)}, u32[]{:S(2)}) collective-permute-start(bf16[512,256]{1,0:T(8,128)(2,1)S(1)} %bitcast.77), channel_id=1, source_target_pairs={{0,4},{4,8},{8,12},{12,16},{16,20},{20,24},{24,28},{28,32},{32,36}... | collective-permute-start | bytes 786440 | tf_op jit(solution)/shard_map/ppermute | solution.py:15
  485.6 1.5 copy-start.6
  560.7 1.7 copy-start
  631.8 4.7 copy-start.2
  631.8 4.7 copy-start.4
  775.2 1.0 copy-start.1
  775.2 791.0 %reduce-scatter.3.cloned.1.call-start = ((), (), s32[]{:S(2)}) async-start(), calls=%async_computation.7 | async-start | bytes 1064960 | tf_op jit(solution)/shard_map/reduce_scatter | solution.py:167
  776.2 8.3 collective-permute-start.3
  777.6 9.7 collective-permute-start.2
  778.9 5.6 copy-start.5
  781.9 5.4 copy-start.3
Sparse Core Ops, SparseCore 0:
  775.3 426.4 reduce-scatter.4
  1204.3 361.9 reduce-scatter.2
where the time goes:
time: 1590 us; the launch traced here: 1570 us
  waiting for transfers between devices  814 us (51%)
  blocking collectives  382 us (24%)
  matrix products  216 us (14%)
  local copies, waits for them, and re-layouts  72.1 us (5%)
  starting transfers between devices  36.3 us (2%)
  other arithmetic  30.7 us (2%)
    reduce_scatter x1, waiting for transfers between devices, shards(): lax.psum_scatter(pvalue_acc, 'ctx', scatter_dimension=0, tiled=True)  414 us
    reduce_scatter x1, waiting for transfers between devices, shards(): lax.psum_scatter(pkey_acc, 'ctx', scatter_dimension=0, tiled=True)  363 us
    all_gather x1, blocking collectives, shards(): lax.all_gather(prefix_keys, 'ctx', axis=0, tiled=True)  195 us
    all_gather x1, blocking collectives, shards(): lax.all_gather(prefix_values, 'ctx', axis=0, tiled=True)  187 us
    dot_general x40, matrix products, one_head(): logits = jnp.dot(query_h, key_h.T, preferred_element_type=jnp.float32)  48.4 us
    dot_general x40, matrix products, one_head(): jnp.dot(weights_b.T, grad_h, preferred_element_type=jnp.float32)  48.2 us
    dot_general x40, matrix products, one_head(): key_term = jnp.dot(dlogits.T, query_h, preferred_element_type=jnp.float32)  47.9 us
    dot_general x40, matrix products, one_head(): dweights = jnp.dot(grad_h, value_h.T, preferred_element_type=jnp.float32)  47.1 us
  transfers between devices with their start and end apart: 11, of which 8 were waited for; matrix products, arithmetic and copies ran while one was open for 2% of the time, Pallas kernels for 0%

commit v1 on v0

--- a/solution.py
+++ b/solution.py
@@ -131,7 +131,9 @@
         shifted(value_two.astype(jnp.bfloat16), "ctx", -1).astype(value_two.dtype),
     )
     whole_keys, whole_values = (
-        lax.all_gather(prefix_keys, "ctx", axis=0, tiled=True),
+        jnp.concatenate(
+            lax.all_to_all(jnp.stack([prefix_keys] * lax.axis_size("ctx")), "ctx", 0, 0), axis=0
+        ),
         lax.all_gather(prefix_values, "ctx", axis=0, tiled=True),
     )
     prompt_total = whole_keys.shape[0]

time: 1590 us -> 1410 us (0.89)
  blocking collectives: 382 us -> 195 us
    all_gather x1 -> x0, blocking collectives: 195 us -> none  [shards(): lax.all_gather(prefix_keys, 'ctx', axis=0, tiled=True)]
  transfers between devices with their start and end apart: 11 -> 12, of which waited for: 8 -> 8; matrix products, arithmetic and copies ran while one was open for 2% -> 13% of each run, Pallas kernels for 0% -> 0%
where the time goes in v1:
time: 1410 us; the launch traced here: 1400 us
  waiting for transfers between devices  819 us (58%)
  matrix products  217 us (15%)
  blocking collectives  195 us (14%)
  local copies, waits for them, and re-layouts  73.7 us (5%)
  starting transfers between devices  44.4 us (3%)
  other arithmetic  30.7 us (2%)
  between operations  14.3 us (1%)
    reduce_scatter x1, waiting for transfers between devices, shards(): lax.psum_scatter(pvalue_acc, 'ctx', scatter_dimension=0, tiled=True)  418 us
    reduce_scatter x1, waiting for transfers between devices, shards(): lax.psum_scatter(pkey_acc, 'ctx', scatter_dimension=0, tiled=True)  363 us
    all_gather x1, blocking collectives, shards(): lax.all_gather(prefix_values, 'ctx', axis=0, tiled=True)  195 us
    dot_general x40, matrix products, one_head(): logits = jnp.dot(query_h, key_h.T, preferred_element_type=jnp.float32)  49.1 us
    dot_general x40, matrix products, one_head(): jnp.dot(weights_b.T, grad_h, preferred_element_type=jnp.float32)  48.2 us
    dot_general x40, matrix products, one_head(): key_term = jnp.dot(dlogits.T, query_h, preferred_element_type=jnp.float32)  47.9 us
    dot_general x40, matrix products, one_head(): dweights = jnp.dot(grad_h, value_h.T, preferred_element_type=jnp.float32)  47.5 us
    dynamic_slice x40, local copies, waits for them, and re-layouts, one_head(): delta_h = lax.dynamic_slice_in_dim(deltas, head, 1, 1)  29.9 us
  transfers between devices with their start and end apart: 12, of which 8 were waited for; matrix products, arithmetic and copies ran while one was open for 13% of the time, Pallas kernels for 0%

profile of v1, /device:TPU:8, one launch (start us, length us, event | category | flops | bytes accessed | tf_op | source)
XLA Modules:
  0.0 1403.0 jit_solution(4384013542308841072)
XLA Ops:
  7.2 1.8 copy.67
  8.9 5.5 all-to-all-start.1
  14.5 1.7 copy.66
  16.2 2.7 all-to-all-done.1
  18.9 5.0 all-to-all-start.3
  23.9 1.4 copy.46
  25.3 2.9 all-to-all-done.3
  28.2 5.3 all-to-all-start.2
  33.5 1.4 copy.50
  35.0 14.2 %all-to-all-done.2 = bf16[128,4,1280]{0,2,1:T(8,128)(2,1)S(1)} async-done(((bf16[128,4,1280]{0,2,1:T(8,128)(2,1)}), bf16[128,4,1280]{0,2,1:T(8,128)(2,1)S(1)}, u32[]{:S(2)}, u32[]{:S(2)}) %all-to-all-start.2) | async-done | bytes 1310752 | tf_op jit(solution)/shard_map/all_to_all | solution.py:99
  49.1 5.3 all-to-all-start.4
  54.8 2.5 copy.65
  57.6 12.4 all-to-all-done.4
  70.0 6.1 all-to-all-start
  76.4 195.1 %all_gather.3 = bf16[1024,256]{1,0:T(8,128)(2,1)} all-gather(bf16[16,256]{1,0:T(8,128)(2,1)S(1)} %copy-done.13), channel_id=1, replica_groups=mesh['ctx'=64,'head'=4] {'ctx'}, dimensions={0}, use_global_device_ids=true | all-gather | bytes 532480 | tf_op jit(solution)/shard_map/all_gather | solution.py:137
  272.9 2.0 collective-permute-start.1
  275.0 6.9 copy.49
  282.0 3.5 reshape.106
  285.4 6.9 copy.51
  292.3 3.5 reshape.107
  295.8 1.5 copy.47
  297.3 2.3 fusion.69
  300.4 11.0 all-to-all-start.5
  312.4 1.7 broadcast.112.clone.1
  314.2 70.8 %while.79 = (s32[]{:T(128)}, f32[512,1280]{1,0:T(8,128)}, f32[512,256]{1,0:T(8,128)S(1)}, f32[512,256]{1,0:T(8,128)S(1)}, bf16[512,1280]{1,0:T(8,128)(2,1)}, /*i...) while((s32[]{:T(128)}, f32[512,1280]{1,0:T(8,128)}, ...), condition=%wide.region_5.6_spmd.clone, body=%wide.region_4.5_spmd.clone.sunk | while | flops 337772544 | bytes 8012191 | solution.py:74
  315.0 1.4 fusion.146
  316.4 1.3 fusion.147
  322.0 1.4 fusion.146
  323.4 1.3 fusion.147
  329.1 1.4 fusion.146
  330.5 1.3 fusion.147
  336.2 1.4 fusion.146
  337.6 1.3 fusion.147
  343.3 1.4 fusion.146
  344.7 1.3 fusion.147
  350.3 1.4 fusion.146
  351.7 1.3 fusion.147
  357.5 1.4 fusion.146
  358.8 1.3 fusion.147
  364.5 1.4 fusion.146
  365.9 1.3 fusion.147
  371.6 1.4 fusion.146
  373.0 1.3 fusion.147
  378.7 1.4 fusion.146
  380.1 1.3 fusion.147
  385.0 1.7 broadcast.112.clone
  386.8 69.1 %while.78 = (s32[]{:T(128)}, f32[512,1280]{1,0:T(8,128)}, f32[512,256]{1,0:T(8,128)S(1)}, f32[512,256]{1,0:T(8,128)S(1)}, bf16[512,1280]{1,0:T(8,128)(2,1)}, /*i...) while((s32[]{:T(128)}, f32[512,1280]{1,0:T(8,128)}, ...), condition=%wide.region_3.4_spmd.clone, body=%wide.region_2.3_spmd.clone.sunk | while | flops 338296832 | bytes 6961531 | solution.py:74
  455.9 4.7 add.320
  462.7 136.6 %while.80 = (s32[]{:T(128)}, f32[512,1280]{1,0:T(8,128)}, f32[1024,256]{1,0:T(8,128)}, f32[1024,256]{1,0:T(8,128)}, bf16[1024,256]{1,0:T(8,128)(2,1)}, /*index=5...) while((s32[]{:T(128)}, f32[512,1280]{1,0:T(8,128)}, ...), condition=%wide.region_15.16_spmd.clone, body=%wide.region_9.15_spmd.clone.sunk | while | flops 85099536 | bytes 14145448 | solution.py:167
  464.1 62.4 %conditional.3 = ((f32[512,1280]{1,0:T(8,128)}, f32[1024,256]{1,0:T(8,128)}, f32[1024,256]{1,0:T(8,128)})) conditional(s32[]{:T(128)} %convert_element_type.143, (f32[512,1280]{1,0:T(8,128)}, f32[1024,256]{1,0:T(8,128)}, f32[1024,256]{1,0:T(8,128)}) %tuple.159, (s32[]{:T(128)}, bf16[1024,256]{1,0:T(8,128)(2,1)}, bf16[1024,256]{1,0:T(8,128)(2,1)}, ...), branch_computations={%region_11.11_spmd, %region_12.14_spmd} | conditional | flops 85098512 | bytes 14136441 | solution.py:165
  466.1 55.2 %while.77 = (s32[]{:T(128)}, f32[512,1280]{1,0:T(8,128)S(1)}, f32[128,256]{1,0:T(8,128)S(1)}, f32[128,256]{1,0:T(8,128)S(1)}, bf16[512,1280]{1,0:T(8,128)(2,1)},...) while((s32[]{:T(128)}, f32[512,1280]{1,0:T(8,128)S(1)}, ...), condition=%wide.region_14.13_spmd.clone, body=%wide.region_13.12_spmd.clone.sunk | while | flops 84377616 | bytes 2339707 | solution.py:74
  521.3 1.7 add_dynamic-update-slice_fusion
  523.0 3.5 add.309
  535.4 62.4 %conditional.3 = ((f32[512,1280]{1,0:T(8,128)}, f32[1024,256]{1,0:T(8,128)}, f32[1024,256]{1,0:T(8,128)})) conditional(s32[]{:T(128)} %convert_element_type.143, (f32[512,1280]{1,0:T(8,128)}, f32[1024,256]{1,0:T(8,128)}, f32[1024,256]{1,0:T(8,128)}) %tuple.159, (s32[]{:T(128)}, bf16[1024,256]{1,0:T(8,128)(2,1)}, bf16[1024,256]{1,0:T(8,128)(2,1)}, ...), branch_computations={%region_11.11_spmd, %region_12.14_spmd} | conditional | flops 85098512 | bytes 14136441 | solution.py:165
  537.3 55.2 %while.77 = (s32[]{:T(128)}, f32[512,1280]{1,0:T(8,128)S(1)}, f32[128,256]{1,0:T(8,128)S(1)}, f32[128,256]{1,0:T(8,128)S(1)}, bf16[512,1280]{1,0:T(8,128)(2,1)},...) while((s32[]{:T(128)}, f32[512,1280]{1,0:T(8,128)S(1)}, ...), condition=%wide.region_14.13_spmd.clone, body=%wide.region_13.12_spmd.clone.sunk | while | flops 84377616 | bytes 2339707 | solution.py:74
  592.5 1.7 add_dynamic-update-slice_fusion
  594.2 3.5 add.309
  603.0 3.1 multiply_convert_fusion
  606.0 2.6 collective-permute-done.3
  609.4 2.0 collective-permute-done.2
  612.2 418.1 %reduce-scatter.5.cloned.1.call-done = f32[16,256]{1,0:T(8,128)} async-done(((f32[1024,256]{1,0:T(8,128)}), f32[16,256]{1,0:T(8,128)}) %reduce-scatter.5.cloned.1.call-update) | async-done | bytes 16400 | tf_op jit(solution)/shard_map/reduce_scatter | solution.py:170
  1030.3 1.3 convert_element_type.106
  1031.6 363.2 %reduce-scatter.3.cloned.1.call-done = f32[16,256]{1,0:T(8,128)} async-done(((f32[1024,256]{1,0:T(8,128)}), f32[16,256]{1,0:T(8,128)}) %reduce-scatter.3.cloned.1.call-update) | async-done | bytes 16400 | tf_op jit(solution)/shard_map/reduce_scatter | solution.py:169
  1394.8 1.3 multiply_convert_fusion.2
  (349 shorter events, 242.0 us)
Async XLA Ops:
  7.2 16.7 %copy-start.11 = (bf16[128,5120]{1,0:T(8,128)(2,1)S(1)}, bf16[128,5120]{1,0:T(8,128)(2,1)}, u32[]{:S(2)}) copy-start(bf16[128,5120]{1,0:T(8,128)(2,1)} %param.24) | copy-start | bytes 3932164
  8.9 9.9 all-to-all-start.1
  18.9 9.4 all-to-all-start.3
  28.2 244.6 %copy-start.7 = (bf16[128,4,256]{2,0,1:T(8,128)(2,1)}, bf16[128,4,256]{2,0,1:T(8,128)(2,1)S(1)}, u32[]{:S(2)}) copy-start(bf16[128,4,256]{2,0,1:T(8,128)(2,1)S(1)} %all-to-all-done.3) | copy-start | bytes 786436
  28.2 5.3 copy-start.12
  28.2 20.9 %all-to-all-start.2 = ((bf16[128,4,1280]{0,2,1:T(8,128)(2,1)}), bf16[128,4,1280]{0,2,1:T(8,128)(2,1)S(1)}, u32[]{:S(2)}, u32[]{:S(2)}) async-start(bf16[128,4,1280]{0,2,1:T(8,128)(2,1)} %bitcast.5), calls=%async_computation.2 | async-start | bytes 2621440 | tf_op jit(solution)/shard_map/all_to_all | solution.py:99
  49.1 5.3 copy-start.16
  49.1 20.9 %all-to-all-start.4 = ((bf16[128,4,1280]{0,2,1:T(8,128)(2,1)}), bf16[128,4,1280]{0,2,1:T(8,128)(2,1)S(1)}, u32[]{:S(2)}, u32[]{:S(2)}) async-start(bf16[128,4,1280]{0,2,1:T(8,128)(2,1)} %bitcast.74), calls=%async_computation.4 | async-start | bytes 2621440 | tf_op jit(solution)/shard_map/all_to_all | solution.py:98
  54.8 2.5 copy-start.15
  70.0 6.4 copy-start.13
  70.0 229.6 %all-to-all-start = ((bf16[128,4,1280]{2,0,1:T(8,128)(2,1)}), bf16[128,4,1280]{2,0,1:T(8,128)(2,1)}, u32[]{:S(2)}, u32[]{:S(2)}) async-start(bf16[128,4,1280]{2,0,1:T(8,128)(2,1)} %bitcast.73), calls=%async_computation | async-start | bytes 2621440 | tf_op jit(solution)/shard_map/all_to_all | solution.py:95
  271.6 40.1 %collective-permute-start = (bf16[512,256]{1,0:T(8,128)(2,1)S(1)}, bf16[512,256]{1,0:T(8,128)(2,1)S(1)}, u32[]{:S(2)}, u32[]{:S(2)}) collective-permute-start(bf16[512,256]{1,0:T(8,128)(2,1)S(1)} %bitcast.76), channel_id=1, source_target_pairs={{0,4},{4,8},{8,12},{12,16},{16,20},{20,24},{24,28},{28,32},{32,36}... | collective-permute-start | bytes 786440 | tf_op jit(solution)/shard_map/ppermute | solution.py:15
  272.9 38.8 %collective-permute-start.1 = (bf16[512,256]{1,0:T(8,128)(2,1)S(1)}, bf16[512,256]{1,0:T(8,128)(2,1)}, u32[]{:S(2)}, u32[]{:S(2)}) collective-permute-start(bf16[512,256]{1,0:T(8,128)(2,1)S(1)} %bitcast.78), channel_id=1, source_target_pairs={{0,4},{4,8},{8,12},{12,16},{16,20},{20,24},{24,28},{28,32},{32,36}... | collective-permute-start | bytes 786440 | tf_op jit(solution)/shard_map/ppermute | solution.py:15
  295.8 1.5 copy-start.6
  297.3 2.3 copy-start.14
  300.4 160.2 %all-to-all-start.5 = ((bf16[64,16,256]{2,1,0:T(8,128)(2,1)}), bf16[64,16,256]{2,1,0:T(8,128)(2,1)}, u32[]{:S(2)}, u32[]{:S(2)}) async-start(bf16[64,16,256]{2,1,0:T(8,128)(2,1)} %stack.2), calls=%async_computation.5 | async-start | bytes 1048576 | tf_op jit(solution)/shard_map/all_to_all | solution.py:135
  311.5 718.9 %reduce-scatter.5.cloned.1.call-start = ((), (), s32[]{:S(2)}) async-start(), calls=%async_computation.9 | async-start | bytes 1064960 | tf_op jit(solution)/shard_map/reduce_scatter | solution.py:170
  311.7 0.7 copy-start.9
  316.4 1.3 copy-start.10
  323.4 1.3 copy-start.10
  330.5 1.3 copy-start.10
  337.6 1.3 copy-start.10
  344.6 1.3 copy-start.10
  351.7 1.3 copy-start.10
  358.8 1.3 copy-start.10
  365.9 1.3 copy-start.10
  373.0 1.3 copy-start.10
  380.1 1.3 copy-start.10
  385.0 1.7 copy-start
  385.0 1.8 copy-start.8
  455.9 4.7 copy-start.2
  455.9 4.7 copy-start.4
  599.3 1.0 copy-start.1
  599.3 795.5 %reduce-scatter.3.cloned.1.call-start = ((), (), s32[]{:S(2)}) async-start(), calls=%async_computation.8 | async-start | bytes 1064960 | tf_op jit(solution)/shard_map/reduce_scatter | solution.py:169
  600.3 8.3 collective-permute-start.3
  601.7 9.7 collective-permute-start.2
  603.0 5.6 copy-start.5
  606.0 5.4 copy-start.3
Sparse Core Ops, SparseCore 0:
  599.4 430.8 reduce-scatter.4
  1032.8 361.9 reduce-scatter.2
